TPU v7x, 128 devices: a whole 4x4x4 slice. The times are simulated.
128 devices in a mesh: ang: 64 (over x, y_lo, z, core), pix: 2 (over y_hi).
Axes of the slice: x: 4, y: 4 (y_hi: 2, y_lo: 2; y = y_hi * 2 + y_lo), z: 4, core: 2. Of those that a mesh axis runs over, the one named last changes fastest.
Arguments:
- grads: bfloat16 [2, 4096, 128, 512], P(None, 'ang', 'pix')
- circle_pos: int32 [4096], replicated, may hold values from 0 to 4095, as said below
- harmonics: int32 [256], replicated, may hold values from 0 to 4095, as said below
- support: int32 [128, 512], replicated, may hold values 0 or 1
Outputs:
- update: bfloat16 [2, 4096, 128, 512], P(None, 'ang', 'pix')
- harmonic_rms: float32 [256], replicated
Inputs may be any that keep to these rules, and one draw needn't show every extreme that they name: `circle_pos`: the stored angles form 64 aligned blocks of 64 rows; block b holds the circle positions r_b + 64 * j for j = 0 to 63 in this order, and the 64 values r_b are distinct. `harmonics`: 256 distinct harmonic numbers, among them 0 and 4095.
All inputs are finite; a program needn't handle non-finite values.
Results may differ from a plain program's by a relative error of at most 0.015.
Values may be sent and summed in bfloat16 or wider, within the bound.
No kernel may reach another device: no remote copies, remote signals or barrier semaphores. Data moves between devices by JAX's collectives and lax.ppermute only.
A program may use at most 192 MiB of HBM per device.

v0:
```python
import math
import jax
import jax.numpy as jnp
from jax import lax
from jax.sharding import PartitionSpec as P


def phase_pair(product, modulus):
    radians = (product % modulus).astype(jnp.float32) * (2.0 * math.pi / modulus)
    return (jnp.cos(radians), jnp.sin(radians))


def split_parts(value):
    if value.dtype == jnp.bfloat16:
        return (value,)
    high = value.astype(jnp.bfloat16)
    low = (value - high.astype(jnp.float32)).astype(jnp.bfloat16)
    return (high, low)


def split_einsum(form, left, right):
    left_parts = split_parts(left)
    right_parts = split_parts(right)
    total = None
    for left_rank, left_piece in enumerate(left_parts):
        for right_rank, right_piece in enumerate(right_parts):
            if left_rank + right_rank <= 1:
                term = jnp.einsum(form, left_piece, right_piece, preferred_element_type=jnp.float32)
                total = term if total is None else total + term
    return total


def normalize(coef_re, coef_im, weight, cell_count):
    square_sums = jnp.sum(weight[None, :] * (coef_re * coef_re + coef_im * coef_im), axis=1)
    totals = lax.psum(square_sums, ("ang", "pix"))
    harmonic_rms = jnp.sqrt(totals / cell_count + 1e-06)
    factor = weight[None, :] / harmonic_rms[:, None]
    return (coef_re * factor, coef_im * factor, harmonic_rms)


def direct_path(grads, circle_pos, harmonics, weight, cell_count):
    angle_count = circle_pos.shape[0]
    kept_count = harmonics.shape[0]
    moved = lax.all_to_all(grads, "ang", split_axis=2, concat_axis=1, tiled=True)
    row_local = moved.shape[2]
    col_count = moved.shape[3]
    flat = moved.reshape(2, angle_count, row_local * col_count)
    pixel_count = flat.shape[2]
    phase_cos, phase_sin = phase_pair(harmonics[:, None] * circle_pos[None, :], angle_count)
    table = jnp.concatenate((phase_cos, phase_sin), 0)
    products = split_einsum("ka,ap->kp", table, jnp.concatenate((flat[0], flat[1]), 1))
    scale = 1.0 / math.sqrt(angle_count)
    coef_re = (products[:kept_count, :pixel_count] + products[kept_count:, pixel_count:]) * scale
    coef_im = (products[:kept_count, pixel_count:] - products[kept_count:, :pixel_count]) * scale
    step_re, step_im, harmonic_rms = normalize(coef_re, coef_im, weight, cell_count)
    right_side = jnp.concatenate(
        (jnp.concatenate((step_re, -step_im), 0), jnp.concatenate((step_im, step_re), 0)), 1
    )
    synthesis = split_einsum("ka,kp->ap", table, right_side)
    scale_back = 1.0 / math.sqrt(kept_count)
    update = jnp.stack((synthesis[:, :pixel_count], synthesis[:, pixel_count:])) * scale_back
    update = update.astype(jnp.bfloat16).reshape(2, angle_count, row_local, col_count)
    return (lax.all_to_all(update, "ang", split_axis=1, concat_axis=2, tiled=True), harmonic_rms)


def body(grads, circle_pos, harmonics, support):
    ang_count = lax.axis_size("ang")
    row_pix = grads.shape[2]
    row_local = row_pix // ang_count
    col_count = grads.shape[3]
    row_start = lax.axis_index("pix") * row_pix + lax.axis_index("ang") * row_local
    weight = (
        lax.dynamic_slice_in_dim(support, row_start, row_local, 0).astype(jnp.float32).reshape(-1)
    )
    cell_count = float(row_pix * lax.axis_size("pix") * col_count)
    update, harmonic_rms = direct_path(grads, circle_pos, harmonics, weight, cell_count)
    return (update, harmonic_rms)


def solution(mesh):
    placed = (P(None, "ang", "pix", None), P(), P(), P())
    return jax.shard_map(
        body,
        mesh=mesh,
        in_specs=placed,
        out_specs=(P(None, "ang", "pix", None), P()),
        check_vma=False,
    )
```

profile of v0, /device:TPU:1, one launch (start us, length us, event | category | flops | bytes accessed | tf_op | source)
XLA Modules:
  0.0 437.9 jit_solution(5942899219189294290)
XLA Ops:
  0.6 11.5 %copy.18 = bf16[2,64,64,512]{3,1,0,2:T(8,128)(2,1)} copy(bf16[2,64,64,512]{3,2,1,0:T(8,128)(2,1)} %param.4) | data formatting | bytes 16777216 | tf_op args[0]
  12.1 0.0 copy-start.6
  12.1 0.0 copy-start.8
  12.1 11.2 %all-to-all-start = ((bf16[2,64,64,512]{3,1,0,2:T(8,128)(2,1)}), bf16[2,64,64,512]{3,1,0,2:T(8,128)(2,1)}, u32[]{:S(2)}, u32[]{:S(2)}) async-start(bf16[2,64,64,512]{3,1,0,2:T(8,128)(2,1)} %copy.18), calls=%async_computation | async-start | bytes 16777216 | tf_op jit(solution)/shard_map/all_to_all | solution.py:44
  23.3 0.7 dynamic-slice_convert_fusion
  24.1 0.0 copy-done.6
  24.1 0.0 copy-done.8
  24.1 18.0 %fusion.8 = (f32[256,4096]{1,0:T(8,128)}, f32[256,4096]{1,0:T(8,128)}) fusion(s32[4096]{0:T(1024)S(1)} %copy-done.6, s32[256]{0:T(256)S(1)} %copy-done.8), kind=kLoop, calls=%fused_computation.23 | loop fusion | flops 14680064 | bytes 8406016 | tf_op jit(solution)/shard_map/cos | solution.py:10
  42.1 84.6 %all-to-all-done = bf16[2,64,64,512]{3,1,0,2:T(8,128)(2,1)} async-done(((bf16[2,64,64,512]{3,1,0,2:T(8,128)(2,1)}), bf16[2,64,64,512]{3,1,0,2:T(8,128)(2,1)}, u32[]{:S(2)}, u32[]{:S(2)}) %all-to-all-start) | async-done | bytes 8388640 | tf_op jit(solution)/shard_map/all_to_all | solution.py:44
  126.7 7.9 %copy.24 = bf16[2,64,64,512]{3,1,2,0:T(8,128)(2,1)} copy(bf16[2,64,64,512]{3,1,0,2:T(8,128)(2,1)} %all-to-all-done) | data formatting | bytes 16777216 | tf_op jit(solution)/shard_map/all_to_all | solution.py:44
  134.6 0.0 copy-start
  134.6 0.0 copy-start.2
  134.6 5.4 %fusion.27 = (bf16[1,64,64,1,512]{4,2,1,3,0:T(8,128)(2,1)S(1)}, bf16[1,64,64,1,512]{4,2,1,3,0:T(8,128)(2,1)}) fusion(bf16[2,64,64,1,512]{4,2,1,3,0:T(8,128)(2,1)} %bitcast.17), kind=kLoop, calls=%fused_computation.41 | loop fusion | bytes 16777216 | tf_op jit(solution)/shard_map/slice | solution.py:51
  140.0 0.0 copy-start.5
  140.0 2.1 copy-done.5
  142.1 0.0 copy-done
  142.1 1.5 copy-done.2
  143.6 8.0 %fusion.2 = f32[512,1024]{1,0:T(8,128)} fusion(bf16[4096,512]{1,0:T(8,128)(2,1)} %bitcast.21, bf16[4096,512]{1,0:T(8,128)(2,1)S(1)} %bitcast.19, f32[256,4096]{1,0:T(8,128)S(1)} %copy-done.2, f32[256,4096]{1,0:T(8,128)S(1)} %copy-done), kind=kOutput, calls=%fused_computation.15 | convolution fusion | flops 4322230272 | bytes 18874368 | tf_op jit(solution)/shard_map/ka,ap->kp/dot_general | solution.py:28
  151.6 8.5 %fusion.9 = f32[512,1024]{1,0:T(8,128)S(1)} fusion(f32[512,1024]{1,0:T(8,128)} %fusion.2, bf16[4096,512]{1,0:T(8,128)(2,1)} %bitcast.22, bf16[4096,512]{1,0:T(8,128)(2,1)} %bitcast.20, f32[256,4096]{1,0:T(8,128)S(1)} %copy-done.2, f32[256,4096]{1,0:T(8,128)S(1)} %copy-done), kind=kOutput, calls=%fused_computation.24 | convolution fusion | flops 4320657408 | bytes 20971520 | tf_op jit(solution)/shard_map/ka,ap->kp/dot_general | solution.py:28
  160.1 0.0 copy-start.4
  160.2 1.3 copy-done.4
  161.5 0.2 multiply_reduce_fusion
  161.7 70.5 %psum.7 = f32[256]{0:T(256)S(1)} all-reduce(f32[256]{0:T(256)S(1)} %multiply_reduce_fusion), channel_id=1, replica_groups=mesh['ang'=64,'pix'=2] {'ang','pix'}, use_global_device_ids=true, to_apply=%region_1.2 | all-reduce | flops 256 | bytes 2048 | tf_op jit(solution)/shard_map/psum | solution.py:35
  232.2 0.0 copy-start.7
  232.3 1.7 fusion.26
  234.0 0.0 copy-start.1
  234.0 0.0 copy-start.3
  234.0 12.7 %fusion.11 = f32[4096,1024]{1,0:T(8,128)} fusion(f32[256,512]{1,0:T(8,128)S(1)} %get-tuple-element.12, f32[256,512]{1,0:T(8,128)S(1)} %get-tuple-element.7, f32[256,512]{1,0:T(8,128)S(1)} %get-tuple-element.6, f32[256,4096]{1,0:T(8,128)} %get-tuple-element.14, f32[256,4096]{1,0:T(8,128)} %get-tuple-element.13), kind=kOutput, calls=%fused_computation.26 | convolution fusion | flops 4307025920 | bytes 26738688 | tf_op jit(solution)/shard_map/ka,kp->ap/dot_general | solution.py:28
  246.7 0.0 copy-done.7
  246.7 0.0 copy-done.1
  246.7 0.0 copy-done.3
  246.7 8.2 %fusion.19 = f32[4096,1024]{1,0:T(8,128)} fusion(f32[256,512]{1,0:T(8,128)S(1)} %get-tuple-element.12, f32[256,512]{1,0:T(8,128)S(1)} %get-tuple-element.7, f32[256,512]{1,0:T(8,128)S(1)} %get-tuple-element.6, f32[256,4096]{1,0:T(8,128)S(1)} %copy-done.3, f32[256,4096]{1,0:T(8,128)S(1)} %copy-done.1), kind=kOutput, calls=%fused_computation.39 | convolution fusion | flops 4307550208 | bytes 26738688 | tf_op jit(solution)/shard_map/ka,kp->ap/dot_general | solution.py:28
  254.9 19.3 %add_add_fusion = f32[4096,1024]{1,0:T(8,128)} fusion(f32[4096,1024]{1,0:T(8,128)} %fusion.19, f32[4096,1024]{1,0:T(8,128)} %fusion.11, f32[256,512]{1,0:T(8,128)S(1)} %get-tuple-element.12, f32[256,512]{1,0:T(8,128)S(1)} %get-tuple-element.7, f32[256,512]{1,0:T(8,128)S(1)} %get-tuple-element.6, f32[256,4096]{1,0:T(8,128)} %get-tuple-element.14, ...), kind=kOutput, calls=%fused_computation.2 | convolution fusion | flops 4318035968 | bytes 60293120 | tf_op jit(solution)/shard_map/ka,kp->ap/dot_general | solution.py:28
  274.1 6.9 %slice_bitcast_fusion.1 = (f32[1,4096,1,512]{3,1,2,0:T(8,128)S(1)}, f32[1,4096,1,512]{3,1,2,0:T(8,128)S(1)}) fusion(f32[4096,1024]{1,0:T(8,128)} %add_add_fusion), kind=kLoop, calls=%fused_computation.4 | loop fusion | bytes 33554432 | tf_op jit(solution)/shard_map/stack | solution.py:61
  281.0 2.5 fusion
  283.5 32.6 %copy.20 = bf16[2,4096,1,512]{3,0,2,1:T(2,128)(2,1)S(1)} copy(bf16[2,4096,1,512]{3,1,2,0:T(8,128)(2,1)S(1)} %fusion) | data formatting | bytes 16777216 | tf_op jit(solution)/shard_map/convert_element_type | solution.py:62
  316.2 102.3 %all_to_all.33 = bf16[2,4096,1,512]{3,0,2,1:T(2,128)(2,1)} all-to-all(bf16[2,4096,1,512]{3,0,2,1:T(2,128)(2,1)S(1)} %copy.20), channel_id=1, replica_groups=mesh['ang'=64,'pix'=2] {'ang'}, dimensions={1} | all-to-all | bytes 16777216 | tf_op jit(solution)/shard_map/all_to_all | solution.py:63
  418.4 8.0 %copy.21 = bf16[2,4096,1,512]{3,1,0,2:T(8,128)(2,1)} copy(bf16[2,4096,1,512]{3,0,2,1:T(2,128)(2,1)} %all_to_all.33) | data formatting | bytes 16777216 | tf_op jit(solution)/shard_map/all_to_all | solution.py:63
  426.4 11.5 %copy.22 = bf16[2,64,64,512]{3,2,1,0:T(8,128)(2,1)} copy(bf16[2,64,64,512]{3,1,2,0:T(8,128)(2,1)} %bitcast.18) | data formatting | bytes 16777216
  (1 shorter events, 0.0 us)
Async XLA Ops:
  12.1 11.9 %copy-start.6 = (s32[4096]{0:T(1024)S(1)}, s32[4096]{0:T(1024)}, u32[]{:S(2)}) copy-start(s32[4096]{0:T(1024)} %param.5) | copy-start | bytes 49156
  12.1 11.9 %copy-start.8 = (s32[256]{0:T(256)S(1)}, s32[256]{0:T(256)}, u32[]{:S(2)}) copy-start(s32[256]{0:T(256)} %param.6) | copy-start | bytes 3076
  12.1 114.6 %all-to-all-start = ((bf16[2,64,64,512]{3,1,0,2:T(8,128)(2,1)}), bf16[2,64,64,512]{3,1,0,2:T(8,128)(2,1)}, u32[]{:S(2)}, u32[]{:S(2)}) async-start(bf16[2,64,64,512]{3,1,0,2:T(8,128)(2,1)} %copy.18), calls=%async_computation | async-start | bytes 16777216 | tf_op jit(solution)/shard_map/all_to_all | solution.py:44
  134.6 7.5 %copy-start = (f32[256,4096]{1,0:T(8,128)S(1)}, f32[256,4096]{1,0:T(8,128)}, u32[]{:S(2)}) copy-start(f32[256,4096]{1,0:T(8,128)} %get-tuple-element.13) | copy-start | bytes 12582916
  134.6 9.0 %copy-start.2 = (f32[256,4096]{1,0:T(8,128)S(1)}, f32[256,4096]{1,0:T(8,128)}, u32[]{:S(2)}) copy-start(f32[256,4096]{1,0:T(8,128)} %get-tuple-element.14) | copy-start | bytes 12582916
  140.0 2.1 copy-start.5
  160.1 1.3 copy-start.4
  232.2 14.4 %copy-start.7 = (f32[256]{0:T(256)}, f32[256]{0:T(256)S(1)}, u32[]{:S(2)}) copy-start(f32[256]{0:T(256)S(1)} %add_sqrt_fusion) | copy-start | bytes 3076
  234.0 12.7 %copy-start.1 = (f32[256,4096]{1,0:T(8,128)S(1)}, f32[256,4096]{1,0:T(8,128)}, u32[]{:S(2)}) copy-start(f32[256,4096]{1,0:T(8,128)} %get-tuple-element.13) | copy-start | bytes 12582916
  234.0 12.7 %copy-start.3 = (f32[256,4096]{1,0:T(8,128)S(1)}, f32[256,4096]{1,0:T(8,128)}, u32[]{:S(2)}) copy-start(f32[256,4096]{1,0:T(8,128)} %get-tuple-element.14) | copy-start | bytes 12582916
where the time goes:
time: 438 us
  blocking collectives  173 us (39%)
  local copies, waits for them, and re-layouts  88.7 us (20%)
  waiting for transfers between devices  84.6 us (19%)
  matrix products  56.7 us (13%)
  other arithmetic  23.2 us (5%)
  starting transfers between devices  11.2 us (3%)
    all_to_all x1, blocking collectives, direct_path(): lax.all_to_all(update, 'ang', split_axis=1, concat_axis=2, tiled=True)  102 us
    all_to_all x1, waiting for transfers between devices, direct_path(): lax.all_to_all(grads, 'ang', split_axis=2, concat_axis=1, tiled=True)  84.6 us
    psum x1, blocking collectives, normalize(): totals = lax.psum(square_sums, ('ang', 'pix'))  70.5 us
    dot_general x5, matrix products, split_einsum(): jnp.einsum(form, left_piece, right_piece, preferred_element_type=jnp.floa...  56.7 us
    convert_element_type x1, local copies, waits for them, and re-layouts, direct_path(): update.astype(jnp.bfloat16).reshape(2, angle_count, row_local, col_count)  32.6 us
    unnamed x20, local copies, waits for them, and re-layouts  28 us
    cos x1, other arithmetic, phase_pair(): return (jnp.cos(radians), jnp.sin(radians))  18 us
    all_to_all x1, starting transfers between devices, direct_path(): lax.all_to_all(grads, 'ang', split_axis=2, concat_axis=1, tiled=True)  11.2 us
  transfers between devices with their start and end apart: 1, of which 1 were waited for; matrix products, arithmetic and copies ran while one was open for 4% of the time, Pallas kernels for 0%

commit v1 on v0

--- a/solution.py
+++ b/solution.py
@@ -32,7 +32,7 @@
 
 def normalize(coef_re, coef_im, weight, cell_count):
     square_sums = jnp.sum(weight[None, :] * (coef_re * coef_re + coef_im * coef_im), axis=1)
-    totals = lax.psum(square_sums, ("ang", "pix"))
+    totals = jnp.sum(lax.all_gather(square_sums, ("ang", "pix")), axis=0)
     harmonic_rms = jnp.sqrt(totals / cell_count + 1e-06)
     factor = weight[None, :] / harmonic_rms[:, None]
     return (coef_re * factor, coef_im * factor, harmonic_rms)

time: 438 us -> 688 us (1.57)
  blocking collectives: 173 us -> 422 us
    all_gather x0 -> x1, blocking collectives: none -> 318 us  [normalize(): totals = jnp.sum(lax.all_gather(square_sums, ('ang', 'pix')), axis=0)]
    psum x1 -> x0, blocking collectives: 70.5 us -> none  [normalize(): totals = lax.psum(square_sums, ('ang', 'pix'))]
  transfers between devices with their start and end apart: 1 -> 1, of which waited for: 1 -> 1; matrix products, arithmetic and copies ran while one was open for 4% -> 3% of each run, Pallas kernels for 0% -> 0%
where the time goes in v1:
time: 688 us; the launch traced here: 687 us
  blocking collectives  422 us (61%)
  local copies, waits for them, and re-layouts  88.7 us (13%)
  waiting for transfers between devices  84.6 us (12%)
  matrix products  56.7 us (8%)
  other arithmetic  23.4 us (3%)
  starting transfers between devices  11.2 us (2%)
    all_gather x1, blocking collectives, normalize(): totals = jnp.sum(lax.all_gather(square_sums, ('ang', 'pix')), axis=0)  318 us
    all_to_all x1, blocking collectives, direct_path(): lax.all_to_all(update, 'ang', split_axis=1, concat_axis=2, tiled=True)  104 us
    all_to_all x1, waiting for transfers between devices, direct_path(): lax.all_to_all(grads, 'ang', split_axis=2, concat_axis=1, tiled=True)  84.6 us
    dot_general x5, matrix products, split_einsum(): jnp.einsum(form, left_piece, right_piece, preferred_element_type=jnp.floa...  56.7 us
    convert_element_type x1, local copies, waits for them, and re-layouts, direct_path(): update.astype(jnp.bfloat16).reshape(2, angle_count, row_local, col_count)  32.6 us
    unnamed x20, local copies, waits for them, and re-layouts  28 us
    cos x1, other arithmetic, phase_pair(): return (jnp.cos(radians), jnp.sin(radians))  18 us
  transfers between devices with their start and end apart: 1, of which 1 were waited for; matrix products, arithmetic and copies ran while one was open for 3% of the time, Pallas kernels for 0%

profile of v1, /device:TPU:1, one launch (start us, length us, event | category | flops | bytes accessed | tf_op | source)
XLA Modules:
  0.0 687.3 jit_solution(5113141207960427377)
XLA Ops:
  0.6 11.5 %copy.18 = bf16[2,64,64,512]{3,1,0,2:T(8,128)(2,1)} copy(bf16[2,64,64,512]{3,2,1,0:T(8,128)(2,1)} %param.4) | data formatting | bytes 16777216 | tf_op args[0]
  12.1 0.0 copy-start.6
  12.1 0.0 copy-start.8
  12.1 11.2 %all-to-all-start = ((bf16[2,64,64,512]{3,1,0,2:T(8,128)(2,1)}), bf16[2,64,64,512]{3,1,0,2:T(8,128)(2,1)}, u32[]{:S(2)}, u32[]{:S(2)}) async-start(bf16[2,64,64,512]{3,1,0,2:T(8,128)(2,1)} %copy.18), calls=%async_computation | async-start | bytes 16777216 | tf_op jit(solution)/shard_map/all_to_all | solution.py:44
  23.3 0.7 dynamic-slice_convert_fusion
  24.1 0.0 copy-done.6
  24.1 0.0 copy-done.8
  24.1 18.0 %fusion.8 = (f32[256,4096]{1,0:T(8,128)}, f32[256,4096]{1,0:T(8,128)}) fusion(s32[4096]{0:T(1024)S(1)} %copy-done.6, s32[256]{0:T(256)S(1)} %copy-done.8), kind=kLoop, calls=%fused_computation.23 | loop fusion | flops 14680064 | bytes 8406016 | tf_op jit(solution)/shard_map/cos | solution.py:10
  42.1 84.6 %all-to-all-done = bf16[2,64,64,512]{3,1,0,2:T(8,128)(2,1)} async-done(((bf16[2,64,64,512]{3,1,0,2:T(8,128)(2,1)}), bf16[2,64,64,512]{3,1,0,2:T(8,128)(2,1)}, u32[]{:S(2)}, u32[]{:S(2)}) %all-to-all-start) | async-done | bytes 8388640 | tf_op jit(solution)/shard_map/all_to_all | solution.py:44
  126.7 7.9 %copy.24 = bf16[2,64,64,512]{3,1,2,0:T(8,128)(2,1)} copy(bf16[2,64,64,512]{3,1,0,2:T(8,128)(2,1)} %all-to-all-done) | data formatting | bytes 16777216 | tf_op jit(solution)/shard_map/all_to_all | solution.py:44
  134.6 0.0 copy-start
  134.6 0.0 copy-start.2
  134.6 5.4 fusion.27
  140.0 0.0 copy-start.5
  140.0 2.1 copy-done.5
  142.1 0.0 copy-done
  142.1 1.5 copy-done.2
  143.6 8.0 %fusion.2 = f32[512,1024]{1,0:T(8,128)} fusion(bf16[4096,512]{1,0:T(8,128)(2,1)} %bitcast.22, bf16[4096,512]{1,0:T(8,128)(2,1)S(1)} %bitcast.20, f32[256,4096]{1,0:T(8,128)S(1)} %copy-done.2, f32[256,4096]{1,0:T(8,128)S(1)} %copy-done), kind=kOutput, calls=%fused_computation.15 | convolution fusion | flops 4322230272 | bytes 18874368 | tf_op jit(solution)/shard_map/ka,ap->kp/dot_general | solution.py:28
  151.6 8.5 %fusion.9 = f32[512,1024]{1,0:T(8,128)S(1)} fusion(f32[512,1024]{1,0:T(8,128)} %fusion.2, bf16[4096,512]{1,0:T(8,128)(2,1)} %bitcast.23, bf16[4096,512]{1,0:T(8,128)(2,1)} %bitcast.21, f32[256,4096]{1,0:T(8,128)S(1)} %copy-done.2, f32[256,4096]{1,0:T(8,128)S(1)} %copy-done), kind=kOutput, calls=%fused_computation.24 | convolution fusion | flops 4320657408 | bytes 20971520 | tf_op jit(solution)/shard_map/ka,ap->kp/dot_general | solution.py:28
  160.1 0.0 copy-start.4
  160.2 1.3 copy-done.4
  161.5 0.2 multiply_reduce_fusion
  161.7 317.8 %all-gather.1 = f32[128,1,256]{2,1,0:T(1,128)S(1)} all-gather(f32[1,1,256]{2,1,0:T(1,128)S(1)} %bitcast.26), channel_id=2, replica_groups=mesh['ang'=64,'pix'=2] {'ang','pix'}, dimensions={0}, use_global_device_ids=true | all-gather | bytes 132096 | tf_op jit(solution)/shard_map/all_gather | solution.py:35
  479.5 0.2 reduce_sum.19
  479.6 0.0 copy-start.7
  479.6 1.7 fusion.26
  481.4 0.0 copy-start.1
  481.4 0.0 copy-start.3
  481.4 12.7 %fusion.11 = f32[4096,1024]{1,0:T(8,128)} fusion(f32[256,512]{1,0:T(8,128)S(1)} %get-tuple-element.12, f32[256,512]{1,0:T(8,128)S(1)} %get-tuple-element.7, f32[256,512]{1,0:T(8,128)S(1)} %get-tuple-element.6, f32[256,4096]{1,0:T(8,128)} %get-tuple-element.14, f32[256,4096]{1,0:T(8,128)} %get-tuple-element.13), kind=kOutput, calls=%fused_computation.26 | convolution fusion | flops 4307025920 | bytes 26738688 | tf_op jit(solution)/shard_map/ka,kp->ap/dot_general | solution.py:28
  494.1 0.0 copy-done.7
  494.1 0.0 copy-done.1
  494.1 0.0 copy-done.3
  494.1 8.2 %fusion.19 = f32[4096,1024]{1,0:T(8,128)} fusion(f32[256,512]{1,0:T(8,128)S(1)} %get-tuple-element.12, f32[256,512]{1,0:T(8,128)S(1)} %get-tuple-element.7, f32[256,512]{1,0:T(8,128)S(1)} %get-tuple-element.6, f32[256,4096]{1,0:T(8,128)S(1)} %copy-done.3, f32[256,4096]{1,0:T(8,128)S(1)} %copy-done.1), kind=kOutput, calls=%fused_computation.39 | convolution fusion | flops 4307550208 | bytes 26738688 | tf_op jit(solution)/shard_map/ka,kp->ap/dot_general | solution.py:28
  502.2 19.3 %add_add_fusion = f32[4096,1024]{1,0:T(8,128)} fusion(f32[4096,1024]{1,0:T(8,128)} %fusion.19, f32[4096,1024]{1,0:T(8,128)} %fusion.11, f32[256,512]{1,0:T(8,128)S(1)} %get-tuple-element.12, f32[256,512]{1,0:T(8,128)S(1)} %get-tuple-element.7, f32[256,512]{1,0:T(8,128)S(1)} %get-tuple-element.6, f32[256,4096]{1,0:T(8,128)} %get-tuple-element.14, ...), kind=kOutput, calls=%fused_computation.2 | convolution fusion | flops 4318035968 | bytes 60293120 | tf_op jit(solution)/shard_map/ka,kp->ap/dot_general | solution.py:28
  521.5 6.9 slice_bitcast_fusion.1
  528.4 2.5 fusion
  530.9 32.6 %copy.20 = bf16[2,4096,1,512]{3,0,2,1:T(2,128)(2,1)S(1)} copy(bf16[2,4096,1,512]{3,1,2,0:T(8,128)(2,1)S(1)} %fusion) | data formatting | bytes 16777216 | tf_op jit(solution)/shard_map/convert_element_type | solution.py:62
  563.5 104.3 %all_to_all.33 = bf16[2,4096,1,512]{3,0,2,1:T(2,128)(2,1)} all-to-all(bf16[2,4096,1,512]{3,0,2,1:T(2,128)(2,1)S(1)} %copy.20), channel_id=1, replica_groups=mesh['ang'=64,'pix'=2] {'ang'}, dimensions={1} | all-to-all | bytes 16777216 | tf_op jit(solution)/shard_map/all_to_all | solution.py:63
  667.8 8.0 %copy.21 = bf16[2,4096,1,512]{3,1,0,2:T(8,128)(2,1)} copy(bf16[2,4096,1,512]{3,0,2,1:T(2,128)(2,1)} %all_to_all.33) | data formatting | bytes 16777216 | tf_op jit(solution)/shard_map/all_to_all | solution.py:63
  675.8 11.5 %copy.22 = bf16[2,64,64,512]{3,2,1,0:T(8,128)(2,1)} copy(bf16[2,64,64,512]{3,1,2,0:T(8,128)(2,1)} %bitcast.19) | data formatting | bytes 16777216
  (1 shorter events, 0.0 us)
Async XLA Ops:
  12.1 11.9 %copy-start.6 = (s32[4096]{0:T(1024)S(1)}, s32[4096]{0:T(1024)}, u32[]{:S(2)}) copy-start(s32[4096]{0:T(1024)} %param.5) | copy-start | bytes 49156
  12.1 11.9 %copy-start.8 = (s32[256]{0:T(256)S(1)}, s32[256]{0:T(256)}, u32[]{:S(2)}) copy-start(s32[256]{0:T(256)} %param.6) | copy-start | bytes 3076
  12.1 114.6 %all-to-all-start = ((bf16[2,64,64,512]{3,1,0,2:T(8,128)(2,1)}), bf16[2,64,64,512]{3,1,0,2:T(8,128)(2,1)}, u32[]{:S(2)}, u32[]{:S(2)}) async-start(bf16[2,64,64,512]{3,1,0,2:T(8,128)(2,1)} %copy.18), calls=%async_computation | async-start | bytes 16777216 | tf_op jit(solution)/shard_map/all_to_all | solution.py:44
  134.6 7.5 %copy-start = (f32[256,4096]{1,0:T(8,128)S(1)}, f32[256,4096]{1,0:T(8,128)}, u32[]{:S(2)}) copy-start(f32[256,4096]{1,0:T(8,128)} %get-tuple-element.13) | copy-start | bytes 12582916
  134.6 9.0 %copy-start.2 = (f32[256,4096]{1,0:T(8,128)S(1)}, f32[256,4096]{1,0:T(8,128)}, u32[]{:S(2)}) copy-start(f32[256,4096]{1,0:T(8,128)} %get-tuple-element.14) | copy-start | bytes 12582916
  140.0 2.1 copy-start.5
  160.1 1.3 copy-start.4
  479.6 14.4 %copy-start.7 = (f32[256]{0:T(256)}, f32[256]{0:T(256)S(1)}, u32[]{:S(2)}) copy-start(f32[256]{0:T(256)S(1)} %add_sqrt_fusion) | copy-start | bytes 3076
  481.4 12.7 %copy-start.1 = (f32[256,4096]{1,0:T(8,128)S(1)}, f32[256,4096]{1,0:T(8,128)}, u32[]{:S(2)}) copy-start(f32[256,4096]{1,0:T(8,128)} %get-tuple-element.13) | copy-start | bytes 12582916
  481.4 12.7 %copy-start.3 = (f32[256,4096]{1,0:T(8,128)S(1)}, f32[256,4096]{1,0:T(8,128)}, u32[]{:S(2)}) copy-start(f32[256,4096]{1,0:T(8,128)} %get-tuple-element.14) | copy-start | bytes 12582916
